TPU v7x, 256 devices: a whole 4x4x8 slice. The times are simulated.
256 devices in a mesh: grp: 4 (over y), ex: 8 (over x, core), tp: 8 (over z).
Axes of the slice: x: 4, y: 4, z: 8, core: 2. Of those that a mesh axis runs over, the one named last changes fastest.
Arguments:
- residual: bfloat16 [512, 2, 6144], P(('grp', 'ex'), None, 'tp'), may hold values from -34 to 34
- query_new: bfloat16 [512, 2, 6144], P(('grp', 'ex'), None, 'tp'), may hold values from -5 to 5
- key_new: bfloat16 [512, 2, 1024], P(('grp', 'ex'), None, 'tp'), may hold values from -8 to 8
- value_new: bfloat16 [512, 2, 1024], P(('grp', 'ex'), None, 'tp'), may hold values from -12 to 12
- key_cache: bfloat16 [512, 8, 512, 128], P(('grp', 'ex'), 'tp'), may hold values from -5 to 5
- value_cache: bfloat16 [512, 8, 512, 128], P(('grp', 'ex'), 'tp'), may hold values from -12 to 12
- lengths: int32 [512], P(('grp', 'ex')), may hold values from 128 to 512, as said below
- norm_gain: bfloat16 [6144], P('tp'), may hold values from 0.099609375 to 1.8984375
- router: float32 [6144, 8], P('tp'), may hold values from -0.078125 to 0.078125
- routes: int32 [512, 2, 2], P(('grp', 'ex')), may hold values from 0 to 7, all different within a row; in each aligned block of 32 rows (0 to 31, 32 to 63, ..., all dimensions but the last counted through in order) at most 16 rows name the same one
- w_gate: bfloat16 [8, 6144, 8192], P('ex', None, ('grp', 'tp')), may hold values from -0.078125 to 0.078125
- w_up: bfloat16 [8, 6144, 8192], P('ex', None, ('grp', 'tp')), may hold values from -0.078125 to 0.078125
- w_down: bfloat16 [8, 8192, 6144], P('ex', ('grp', 'tp')), may hold values from -0.125 to 0.125
Outputs:
- attended: bfloat16 [512, 2, 6144], P(('grp', 'ex'), None, 'tp')
- expert_mix: bfloat16 [512, 2, 6144], P(('grp', 'ex'), None, 'tp')
Inputs may be any that keep to these rules, and one draw needn't show every extreme that they name: `routes`: over the rows of one device (aligned blocks of 32 rows, environments then steps) no expert is named more than 16 times, and in some blocks one is named exactly 16 times; a row's two experts differ. `lengths`: some environment's cache is full.
All inputs are finite; a program needn't handle non-finite values.
Results may differ from a plain program's by a relative error of at most 0.023.
Values may be sent and summed in bfloat16 or wider, within the bound.
No kernel may reach another device: no remote copies, remote signals or barrier semaphores. Data moves between devices by JAX's collectives and lax.ppermute only.
A program may use at most 128 MiB of HBM per device.

v0:
```python
import jax
import jax.numpy as jnp
from jax import lax
from jax.sharding import PartitionSpec as P

CAP = 16


def attend(query_new, key_new, value_new, key_cache, value_cache, lengths):
    env_count, step_count, feature_count = query_new.shape
    kv_count = key_cache.shape[1]
    context = key_cache.shape[2]
    head_dim = key_cache.shape[3]
    group_size = feature_count // (kv_count * head_dim)
    queries = query_new.reshape(env_count, step_count, kv_count, group_size, head_dim)
    keys_now = key_new.reshape(env_count, step_count, kv_count, head_dim)
    values_now = value_new.reshape(env_count, step_count, kv_count, head_dim)
    score_scale = head_dim ** (-0.5)
    cached = (
        jnp.einsum("eskgd,ekcd->eskgc", queries, key_cache, preferred_element_type=jnp.float32)
        * score_scale
    )
    fresh_scores = (
        jnp.einsum("eskgd,etkd->eskgt", queries, keys_now, preferred_element_type=jnp.float32)
        * score_scale
    )
    valid_mask = (lax.broadcasted_iota(jnp.int32, (env_count, context), 1) < lengths[:, None])[
        :, None, None, None, :
    ]
    causal = (
        lax.broadcasted_iota(jnp.int32, (step_count, step_count), 1)
        <= lax.broadcasted_iota(jnp.int32, (step_count, step_count), 0)
    )[None, :, None, None, :]
    cached = jnp.where(valid_mask, cached, -1e30)
    fresh_scores = jnp.where(causal, fresh_scores, -1e30)
    row_top = jnp.maximum(jnp.max(cached, -1), jnp.max(fresh_scores, -1))[..., None]
    weight_cached = jnp.where(valid_mask, jnp.exp(cached - row_top), 0.0)
    weight_fresh = jnp.where(causal, jnp.exp(fresh_scores - row_top), 0.0)
    row_total = (jnp.sum(weight_cached, -1) + jnp.sum(weight_fresh, -1))[..., None]
    probs_cached = (weight_cached / row_total).astype(jnp.bfloat16)
    probs_fresh = (weight_fresh / row_total).astype(jnp.bfloat16)
    heads_out = jnp.einsum(
        "eskgc,ekcd->eskgd", probs_cached, value_cache, preferred_element_type=jnp.float32
    )
    heads_out = heads_out + jnp.einsum(
        "eskgt,etkd->eskgd", probs_fresh, values_now, preferred_element_type=jnp.float32
    )
    return heads_out.reshape(env_count, step_count, feature_count)


def per_device(
    residual,
    query_new,
    key_new,
    value_new,
    key_cache,
    value_cache,
    lengths,
    norm_gain,
    router,
    routes,
    w_gate,
    w_up,
    w_down,
):
    env_count, step_count, slice_width = residual.shape
    local_experts, width, hidden_local = w_gate.shape
    experts = router.shape[1]
    topk = routes.shape[2]
    group_count = lax.axis_size("grp")
    tensor_count = lax.axis_size("tp")
    owner_count = lax.axis_size("ex")
    row_count = env_count * step_count
    state = residual.astype(jnp.float32) + attend(
        query_new, key_new, value_new, key_cache, value_cache, lengths
    )
    attended = state.astype(jnp.bfloat16)
    squares = jnp.sum(state * state, -1)
    scaled = state * norm_gain.astype(jnp.float32)
    partial_logits = jnp.einsum("esd,dx->esx", scaled, router, precision=lax.Precision.HIGHEST)
    squares, logits = lax.psum((squares, partial_logits), "tp")
    root_mean = jnp.sqrt(squares / width + 1e-05)[..., None]
    logits = logits / root_mean
    normed = (scaled / root_mean).astype(jnp.bfloat16)
    expert_ids = lax.broadcasted_iota(jnp.int32, (1, 1, 1, experts), 3)
    picked_logits = jnp.sum(
        jnp.where(routes[..., None] == expert_ids, logits[:, :, None, :], 0.0), -1
    )
    first_gate = 1.0 / (1.0 + jnp.exp(picked_logits[..., 1] - picked_logits[..., 0]))
    second_gate = 1.0 - first_gate
    flat_routes = routes.reshape(row_count * topk)
    expert_hits = (flat_routes[:, None] == lax.broadcasted_iota(jnp.int32, (1, experts), 1)).astype(
        jnp.int32
    )
    earlier = jnp.cumsum(expert_hits, axis=0) - expert_hits
    slot_ids = jnp.sum(earlier * expert_hits, axis=1)
    targets = flat_routes * CAP + slot_ids
    slot_table = lax.broadcasted_iota(jnp.int32, (1, experts * CAP), 1)
    placed = (
        (targets[:, None] == slot_table)
        .astype(jnp.bfloat16)
        .reshape(row_count, topk, experts * CAP)
    )
    sender = jnp.sum(placed, axis=1)
    packed = jnp.einsum(
        "rs,rd->sd",
        sender,
        normed.reshape(row_count, slice_width),
        preferred_element_type=jnp.float32,
    )
    outgoing = packed.astype(jnp.bfloat16).reshape(experts, CAP, slice_width)
    received = lax.all_to_all(outgoing, "ex", split_axis=0, concat_axis=0, tiled=True)
    received = received.reshape(1, owner_count, local_experts, CAP, slice_width)
    pieces = lax.all_gather(received, ("grp", "tp"), axis=0, tiled=True)
    pieces = pieces.reshape(group_count, tensor_count, owner_count, local_experts, CAP, slice_width)
    gate_split = w_gate.reshape(local_experts, tensor_count, slice_width, hidden_local)
    up_split = w_up.reshape(local_experts, tensor_count, slice_width, hidden_local)
    gate_sums = jnp.einsum(
        "gtajcd,jtdf->jgacf", pieces, gate_split, preferred_element_type=jnp.float32
    )
    up_sums = jnp.einsum("gtajcd,jtdf->jgacf", pieces, up_split, preferred_element_type=jnp.float32)
    hidden = (jax.nn.silu(gate_sums) * up_sums).astype(jnp.bfloat16)
    down_split = w_down.reshape(local_experts, hidden_local, tensor_count, slice_width)
    down_terms = jnp.einsum(
        "jgacf,jftd->gtajcd", hidden, down_split, preferred_element_type=jnp.float32
    )
    down_terms = down_terms.reshape(
        group_count * tensor_count, owner_count, local_experts, CAP, slice_width
    )
    summed = lax.psum_scatter(
        down_terms.astype(jnp.bfloat16), ("grp", "tp"), scatter_dimension=0, tiled=True
    ).astype(jnp.float32)
    returned = lax.all_to_all(
        summed[0].astype(jnp.bfloat16), "ex", split_axis=0, concat_axis=0, tiled=True
    )
    returned = returned.reshape(experts * CAP, slice_width)
    picked_rows = jnp.einsum("rks,sd->rkd", placed, returned, preferred_element_type=jnp.float32)
    picked_rows = picked_rows.reshape(env_count, step_count, topk, slice_width)
    expert_mix = (
        first_gate[..., None] * picked_rows[:, :, 0] + second_gate[..., None] * picked_rows[:, :, 1]
    )
    return (attended, expert_mix.astype(jnp.bfloat16))


def solution(mesh):
    return jax.shard_map(
        per_device,
        mesh=mesh,
        in_specs=(
            P(("grp", "ex"), None, "tp"),
            P(("grp", "ex"), None, "tp"),
            P(("grp", "ex"), None, "tp"),
            P(("grp", "ex"), None, "tp"),
            P(("grp", "ex"), "tp", None, None),
            P(("grp", "ex"), "tp", None, None),
            P(("grp", "ex")),
            P("tp"),
            P("tp", None),
            P(("grp", "ex"), None, None),
            P("ex", None, ("grp", "tp")),
            P("ex", None, ("grp", "tp")),
            P("ex", ("grp", "tp"), None),
        ),
        out_specs=(P(("grp", "ex"), None, "tp"), P(("grp", "ex"), None, "tp")),
        check_vma=False,
    )
```

profile of v0, /device:TPU:1, one launch (start us, length us, event | category | flops | bytes accessed | tf_op | source)
XLA Modules:
  0.0 389.3 jit_solution(13137319937710696107)
XLA Ops:
  7.2 0.8 broadcast_multiply_fusion
  8.1 0.8 copy.92
  8.9 0.8 reshape.262
  9.8 0.9 iota_compare_fusion.3
  10.6 2.3 fusion.55
  13.0 1.1 fusion.56
  14.2 0.3 fusion.28
  14.5 0.1 fusion.50
  14.6 0.3 fusion.46
  14.9 0.5 fusion.23
  15.6 0.5 fusion.37
  16.1 17.7 %all-reduce = (f32[16,2]{0,1:T(2,128)S(1)}, f32[16,2,8]{0,2,1:T(8,128)S(1)}) all-reduce(f32[16,2]{0,1:T(2,128)S(1)} %multiply_reduce_fusion, f32[16,2,8]{0,2,1:T(8,128)S(1)} %fusion.37), channel_id=1, replica_groups=mesh['grp'=4,'ex'=8,'tp'=8] {'tp'}, use_global_device_ids=true, to_apply=%region_6.7 | all-reduce | flops 288 | bytes 2304 | tf_op jit(solution)/shard_map/psum | solution.py:81
  34.1 0.1 eq.68
  34.3 0.1 reduce_window_sum.11
  34.4 0.2 select_reduce_fusion
  34.6 0.1 reduce_sum.64
  34.9 0.2 convolution_convert_fusion
  35.2 14.4 %all_to_all.10 = bf16[8,16,768]{2,1,0:T(8,128)(2,1)} all-to-all(bf16[8,16,768]{2,1,0:T(8,128)(2,1)S(1)} %bitcast.164), channel_id=1, replica_groups=mesh['grp'=4,'ex'=8,'tp'=8] {'ex'}, dimensions={0} | all-to-all | bytes 393216 | tf_op jit(solution)/shard_map/all_to_all | solution.py:112
  49.6 4.5 %copy.120 = bf16[32,8,8,768]{3,2,1,0:T(8,128)(2,1)} copy(bf16[32,8,8,768]{3,1,2,0:T(8,128)(2,1)} %bitcast.162) | data formatting | bytes 6291456
  54.1 79.5 %all-gather.3.cloned.1.call-done = bf16[256,16,768]{2,1,0:T(8,128)(2,1)} async-done(((bf16[8,16,768]{2,1,0:T(8,128)(2,1)}), bf16[256,16,768]{2,1,0:T(8,128)(2,1)}) %all-gather.3.cloned.1.call-update) | async-done | bytes 6291472 | tf_op jit(solution)/shard_map/all_gather | solution.py:114
  133.6 4.7 %convolution_bitcast_fusion.1 = f32[4,8,16,256]{3,2,1,0:T(8,128)S(1)} fusion(bf16[4,8,8,16,768]{4,3,2,1,0:T(8,128)(2,1)} %bitcast.168, bf16[8,768,256,1,1]{2,1,4,0,3:T(8,128)(2,1)S(1)} %bitcast.159), kind=kOutput, calls=%fused_computation.8 | convolution fusion | flops 1610612736 | bytes 9961472 | tf_op jit(solution)/shard_map/gtajcd,jtdf->jgacf/dot_general | solution.py:118
  138.3 0.8 copy-done.7
  139.1 1.8 fusion.19
  140.9 0.1 copy-done.1
  141.0 1.9 convert_bitcast_fusion
  142.9 3.5 copy.98
  146.5 0.7 copy.102
  147.3 219.0 %reduce-scatter.2.cloned.1.call-done = bf16[1,8,1,16,768]{4,3,1,0,2:T(8,128)(2,1)} async-done(((bf16[32,8,1,16,768]{4,3,1,0,2:T(8,128)(2,1)}), bf16[1,8,1,16,768]{4,3,1,0,2:T(8,128)(2,1)}) %reduce-scatter.2.cloned.1.call-update) | async-done | bytes 196624 | tf_op jit(solution)/shard_map/reduce_scatter | solution.py:130
  366.3 9.4 %all-to-all-start.1 = ((bf16[8,1,16,768]{3,2,1,0:T(8,128)(2,1)}), bf16[8,1,16,768]{3,2,1,0:T(8,128)(2,1)S(1)}, u32[]{:S(2)}, u32[]{:S(2)}) async-start(bf16[8,1,16,768]{3,2,1,0:T(8,128)(2,1)} %bitcast.165), calls=%async_computation.2 | async-start | bytes 393216 | tf_op jit(solution)/shard_map/all_to_all | solution.py:133
  375.7 5.8 %all-to-all-done.1 = bf16[8,1,16,768]{3,2,1,0:T(8,128)(2,1)S(1)} async-done(((bf16[8,1,16,768]{3,2,1,0:T(8,128)(2,1)}), bf16[8,1,16,768]{3,2,1,0:T(8,128)(2,1)S(1)}, u32[]{:S(2)}, u32[]{:S(2)}) %all-to-all-start.1) | async-done | bytes 196640 | tf_op jit(solution)/shard_map/all_to_all | solution.py:133
  381.6 0.2 fusion.42
  381.8 0.7 copy.103
  (44 shorter events, 1.1 us)
Async XLA Ops:
  7.2 126.4 %copy-start = (bf16[1,6144,256]{2,1,0:T(8,128)(2,1)S(1)}, bf16[1,6144,256]{2,1,0:T(8,128)(2,1)}, u32[]{:S(2)}) copy-start(bf16[1,6144,256]{2,1,0:T(8,128)(2,1)} %param.23) | copy-start | bytes 9437188
  7.2 7.4 %copy-start.9 = (bf16[16,2,128]{2,1,0:T(2,128)(2,1)S(1)}, bf16[16,2,128]{2,1,0:T(2,128)(2,1)}, u32[]{:S(2)}) copy-start(bf16[16,2,128]{2,1,0:T(2,128)(2,1)} %param.16) | copy-start | bytes 24580
  7.2 126.4 %all-gather.3.cloned.1.call-start = ((), (), s32[]{:S(2)}) async-start(), calls=%async_computation.4 | async-start | bytes 6488064 | tf_op jit(solution)/shard_map/all_gather | solution.py:114
  9.8 5.2 %copy-start.8 = (bf16[16,1,512,128]{3,2,1,0:T(8,128)(2,1)S(1)}, bf16[16,1,512,128]{3,2,1,0:T(8,128)(2,1)}, u32[]{:S(2)}) copy-start(bf16[16,1,512,128]{3,2,1,0:T(8,128)(2,1)} %param.18) | copy-start | bytes 6291460
  13.0 2.5 copy-start.5
  13.0 2.5 copy-start.2
  13.0 2.6 copy-start.3
  49.5 316.7 %reduce-scatter.2.cloned.1.call-start = ((), (), s32[]{:S(2)}) async-start(), calls=%async_computation.3 | async-start | bytes 6488064 | tf_op jit(solution)/shard_map/reduce_scatter | solution.py:130
  133.6 4.7 %copy-start.6 = (bf16[256,16,768]{2,1,0:T(8,128)(2,1)S(1)}, bf16[256,16,768]{2,1,0:T(8,128)(2,1)}, u32[]{:S(2)}) copy-start(bf16[256,16,768]{2,1,0:T(8,128)(2,1)} %all-gather.3.cloned.1.call-done) | copy-start | bytes 18874372
  133.6 5.5 %copy-start.7 = (bf16[1,6144,256]{2,1,0:T(8,128)(2,1)S(1)}, bf16[1,6144,256]{2,1,0:T(8,128)(2,1)}, u32[]{:S(2)}) copy-start(bf16[1,6144,256]{2,1,0:T(8,128)(2,1)} %param.24) | copy-start | bytes 9437188
  139.1 1.9 copy-start.1
  146.5 0.8 copy-start.4
  366.3 15.3 %all-to-all-start.1 = ((bf16[8,1,16,768]{3,2,1,0:T(8,128)(2,1)}), bf16[8,1,16,768]{3,2,1,0:T(8,128)(2,1)S(1)}, u32[]{:S(2)}, u32[]{:S(2)}) async-start(bf16[8,1,16,768]{3,2,1,0:T(8,128)(2,1)} %bitcast.165), calls=%async_computation.2 | async-start | bytes 393216 | tf_op jit(solution)/shard_map/all_to_all | solution.py:133
Sparse Core Ops, SparseCore 0:
  49.7 83.8 all-gather.2
  146.6 219.6 reduce-scatter.1
where the time goes:
time: 390 us; the launch traced here: 389 us
  waiting for transfers between devices  304 us (78%)
  blocking collectives  32 us (8%)
  between operations  14.3 us (4%)
  matrix products  13.5 us (3%)
  local copies, waits for them, and re-layouts  12.6 us (3%)
  starting transfers between devices  9.5 us (2%)
    reduce_scatter x1, waiting for transfers between devices, per_device(): lax.psum_scatter(down_terms.astype(jnp.bfloat16), ('grp', 'tp'), scatter_...  219 us
    all_gather x1, waiting for transfers between devices, per_device(): pieces = lax.all_gather(received, ('grp', 'tp'), axis=0, tiled=True)  79.5 us
    psum x1, blocking collectives, per_device(): squares, logits = lax.psum((squares, partial_logits), 'tp')  17.7 us
    all_to_all x1, blocking collectives, per_device(): lax.all_to_all(outgoing, 'ex', split_axis=0, concat_axis=0, tiled=True)  14.4 us
    all_to_all x1, starting transfers between devices, per_device(): lax.all_to_all(summed[0].astype(jnp.bfloat16), 'ex', split_axis=0, concat...  9.42 us
  transfers between devices with their start and end apart: 3, of which 3 were waited for; matrix products, arithmetic and copies ran while one was open for 1% of the time, Pallas kernels for 0%

commit v1 on v0

--- a/solution.py
+++ b/solution.py
@@ -111,7 +111,10 @@
     outgoing = packed.astype(jnp.bfloat16).reshape(experts, CAP, slice_width)
     received = lax.all_to_all(outgoing, "ex", split_axis=0, concat_axis=0, tiled=True)
     received = received.reshape(1, owner_count, local_experts, CAP, slice_width)
-    pieces = lax.all_gather(received, ("grp", "tp"), axis=0, tiled=True)
+    pieces = jnp.concatenate(
+        lax.all_to_all(jnp.stack([received] * lax.axis_size(("grp", "tp"))), ("grp", "tp"), 0, 0),
+        axis=0,
+    )
     pieces = pieces.reshape(group_count, tensor_count, owner_count, local_experts, CAP, slice_width)
     gate_split = w_gate.reshape(local_experts, tensor_count, slice_width, hidden_local)
     up_split = w_up.reshape(local_experts, tensor_count, slice_width, hidden_local)

time: 390 us -> 457 us (1.17)
  waiting for transfers between devices: 304 us -> 360 us
  starting transfers between devices: 9.5 us -> 15.9 us
    all_to_all x0 -> x1, waiting for transfers between devices: none -> 136 us  [per_device(): lax.all_to_all(jnp.stack([received] * lax.axis_size(('grp', 'tp'))), ('gr...]
    all_gather x1 -> x0, waiting for transfers between devices: 79.5 us -> none  [per_device(): pieces = lax.all_gather(received, ('grp', 'tp'), axis=0, tiled=True)]
    all_to_all x0 -> x1, starting transfers between devices: none -> 6.49 us  [per_device(): lax.all_to_all(jnp.stack([received] * lax.axis_size(('grp', 'tp'))), ('gr...]
where the time goes in v1:
time: 457 us
  waiting for transfers between devices  360 us (79%)
  blocking collectives  31.9 us (7%)
  matrix products  16.5 us (4%)
  starting transfers between devices  15.9 us (3%)
  local copies, waits for them, and re-layouts  15.1 us (3%)
  between operations  14.3 us (3%)
    reduce_scatter x1, waiting for transfers between devices, per_device(): lax.psum_scatter(down_terms.astype(jnp.bfloat16), ('grp', 'tp'), scatter_...  218 us
    all_to_all x1, waiting for transfers between devices, per_device(): lax.all_to_all(jnp.stack([received] * lax.axis_size(('grp', 'tp'))), ('gr...  136 us
    psum x1, blocking collectives, per_device(): squares, logits = lax.psum((squares, partial_logits), 'tp')  17.7 us
    all_to_all x1, blocking collectives, per_device(): lax.all_to_all(outgoing, 'ex', split_axis=0, concat_axis=0, tiled=True)  14.2 us
    all_to_all x1, starting transfers between devices, per_device(): lax.all_to_all(summed[0].astype(jnp.bfloat16), 'ex', split_axis=0, concat...  9.39 us
  transfers between devices with their start and end apart: 3, of which 3 were waited for; matrix products, arithmetic and copies ran while one was open for 1% of the time, Pallas kernels for 0%

profile of v1, /device:TPU:1, one launch (start us, length us, event | category | flops | bytes accessed | tf_op | source)
XLA Modules:
  0.0 456.8 jit_solution(5945550306415619645)
XLA Ops:
  7.2 0.8 broadcast_multiply_fusion
  8.0 0.9 copy.92
  8.9 0.8 reshape.257
  9.8 0.9 iota_compare_fusion.3
  10.6 2.3 fusion.55
  13.0 1.1 fusion.56
  14.2 0.3 fusion.28
  14.5 0.1 fusion.50
  14.6 0.3 fusion.46
  14.9 0.5 fusion.23
  15.7 0.5 fusion.37
  16.1 17.7 %all-reduce = (f32[16,2]{0,1:T(2,128)S(1)}, f32[16,2,8]{0,2,1:T(8,128)S(1)}) all-reduce(f32[16,2]{0,1:T(2,128)S(1)} %multiply_reduce_fusion, f32[16,2,8]{0,2,1:T(8,128)S(1)} %fusion.37), channel_id=1, replica_groups=mesh['grp'=4,'ex'=8,'tp'=8] {'tp'}, use_global_device_ids=true, to_apply=%region_6.7 | all-reduce | flops 288 | bytes 2304 | tf_op jit(solution)/shard_map/psum | solution.py:81
  34.1 0.1 eq.68
  34.3 0.1 reduce_window_sum.11
  34.4 0.2 select_reduce_fusion
  34.6 0.1 reduce_sum.64
  34.9 0.2 convolution_convert_fusion
  35.2 14.2 %all_to_all.15 = bf16[8,16,768]{2,1,0:T(8,128)(2,1)S(1)} all-to-all(bf16[8,16,768]{2,1,0:T(8,128)(2,1)S(1)} %bitcast.164), channel_id=1, replica_groups=mesh['grp'=4,'ex'=8,'tp'=8] {'ex'}, dimensions={0} | all-to-all | bytes 393216 | tf_op jit(solution)/shard_map/all_to_all | solution.py:112
  49.4 3.4 stack.3
  52.8 6.5 %all-to-all-start.1 = ((bf16[32,1,8,1,16,768]{5,4,2,3,1,0:T(8,128)(2,1)}), bf16[32,1,8,1,16,768]{5,4,2,3,1,0:T(8,128)(2,1)}, u32[]{:S(2)}, u32[]{:S(2)}) async-start(bf16[32,1,8,1,16,768]{5,4,2,3,1,0:T(8,128)(2,1)} %stack.3), calls=%async_computation.1 | async-start | bytes 12582912 | tf_op jit(solution)/shard_map/all_to_all | solution.py:115
  59.3 4.5 copy.120
  63.8 135.9 %all-to-all-done.1 = bf16[32,1,8,1,16,768]{5,4,2,3,1,0:T(8,128)(2,1)} async-done(((bf16[32,1,8,1,16,768]{5,4,2,3,1,0:T(8,128)(2,1)}), bf16[32,1,8,1,16,768]{5,4,2,3,1,0:T(8,128)(2,1)}, u32[]{:S(2)}, u32[]{:S(2)}) %all-to-all-start.1) | async-done | bytes 6291488 | tf_op jit(solution)/shard_map/all_to_all | solution.py:115
  199.7 4.7 %convolution_bitcast_fusion.1 = f32[4,8,16,256]{3,2,1,0:T(8,128)S(1)} fusion(bf16[4,8,8,16,768]{4,3,2,1,0:T(8,128)(2,1)} %bitcast.22, bf16[8,768,256,1,1]{2,1,4,0,3:T(8,128)(2,1)S(1)} %bitcast.159), kind=kOutput, calls=%fused_computation.8 | convolution fusion | flops 1610612736 | bytes 9961472 | tf_op jit(solution)/shard_map/gtajcd,jtdf->jgacf/dot_general | solution.py:121
  204.4 4.7 %fusion.19 = bf16[4,8,16,256,1]{3,2,4,1,0:T(8,128)(2,1)S(1)} fusion(bf16[4,8,8,16,768]{4,3,2,1,0:T(8,128)(2,1)} %bitcast.22, bf16[8,768,256,1,1]{2,1,4,0,3:T(8,128)(2,1)S(1)} %bitcast.168, f32[4,8,16,256]{3,2,1,0:T(8,128)S(1)} %convolution_bitcast_fusion.1), kind=kOutput, calls=%fused_computation.15 | convolution fusion | flops 1611399168 | bytes 10223616 | tf_op jit(solution)/shard_map/gtajcd,jtdf->jgacf/dot_general | solution.py:124
  209.1 1.9 convert_bitcast_fusion
  211.1 3.5 copy.98
  214.7 0.7 copy.102
  215.5 218.4 %reduce-scatter.2.cloned.1.call-done = bf16[1,8,1,16,768]{4,3,1,0,2:T(8,128)(2,1)} async-done(((bf16[32,8,1,16,768]{4,3,1,0,2:T(8,128)(2,1)}), bf16[1,8,1,16,768]{4,3,1,0,2:T(8,128)(2,1)}) %reduce-scatter.2.cloned.1.call-update) | async-done | bytes 196624 | tf_op jit(solution)/shard_map/reduce_scatter | solution.py:133
  433.8 9.4 %all-to-all-start.2 = ((bf16[8,1,16,768]{3,2,1,0:T(8,128)(2,1)}), bf16[8,1,16,768]{3,2,1,0:T(8,128)(2,1)S(1)}, u32[]{:S(2)}, u32[]{:S(2)}) async-start(bf16[8,1,16,768]{3,2,1,0:T(8,128)(2,1)} %bitcast.165), calls=%async_computation.3 | async-start | bytes 393216 | tf_op jit(solution)/shard_map/all_to_all | solution.py:136
  443.2 5.8 %all-to-all-done.2 = bf16[8,1,16,768]{3,2,1,0:T(8,128)(2,1)S(1)} async-done(((bf16[8,1,16,768]{3,2,1,0:T(8,128)(2,1)}), bf16[8,1,16,768]{3,2,1,0:T(8,128)(2,1)S(1)}, u32[]{:S(2)}, u32[]{:S(2)}) %all-to-all-start.2) | async-done | bytes 196640 | tf_op jit(solution)/shard_map/all_to_all | solution.py:136
  449.1 0.2 fusion.42
  449.3 0.7 copy.103
  (42 shorter events, 1.1 us)
Async XLA Ops:
  7.2 192.5 %copy-start = (bf16[1,6144,256]{2,1,0:T(8,128)(2,1)S(1)}, bf16[1,6144,256]{2,1,0:T(8,128)(2,1)}, u32[]{:S(2)}) copy-start(bf16[1,6144,256]{2,1,0:T(8,128)(2,1)} %param.23) | copy-start | bytes 9437188
  7.2 7.4 %copy-start.8 = (bf16[16,2,128]{2,1,0:T(2,128)(2,1)S(1)}, bf16[16,2,128]{2,1,0:T(2,128)(2,1)}, u32[]{:S(2)}) copy-start(bf16[16,2,128]{2,1,0:T(2,128)(2,1)} %param.16) | copy-start | bytes 24580
  9.8 5.2 %copy-start.7 = (bf16[16,1,512,128]{3,2,1,0:T(8,128)(2,1)S(1)}, bf16[16,1,512,128]{3,2,1,0:T(8,128)(2,1)}, u32[]{:S(2)}) copy-start(bf16[16,1,512,128]{3,2,1,0:T(8,128)(2,1)} %param.18) | copy-start | bytes 6291460
  13.0 2.5 copy-start.5
  13.0 2.5 copy-start.2
  13.0 2.6 copy-start.3
  52.8 146.9 %all-to-all-start.1 = ((bf16[32,1,8,1,16,768]{5,4,2,3,1,0:T(8,128)(2,1)}), bf16[32,1,8,1,16,768]{5,4,2,3,1,0:T(8,128)(2,1)}, u32[]{:S(2)}, u32[]{:S(2)}) async-start(bf16[32,1,8,1,16,768]{5,4,2,3,1,0:T(8,128)(2,1)} %stack.3), calls=%async_computation.1 | async-start | bytes 12582912 | tf_op jit(solution)/shard_map/all_to_all | solution.py:115
  59.3 374.5 %reduce-scatter.2.cloned.1.call-start = ((), (), s32[]{:S(2)}) async-start(), calls=%async_computation.4 | async-start | bytes 6488064 | tf_op jit(solution)/shard_map/reduce_scatter | solution.py:133
  199.7 4.7 %copy-start.6 = (bf16[1,6144,256]{2,1,0:T(8,128)(2,1)S(1)}, bf16[1,6144,256]{2,1,0:T(8,128)(2,1)}, u32[]{:S(2)}) copy-start(bf16[1,6144,256]{2,1,0:T(8,128)(2,1)} %param.24) | copy-start | bytes 9437188
  204.4 4.7 %copy-start.1 = (bf16[32,8,8,768]{3,2,1,0:T(8,128)(2,1)S(1)}, bf16[32,8,8,768]{3,2,1,0:T(8,128)(2,1)}, u32[]{:S(2)}) copy-start(bf16[32,8,8,768]{3,2,1,0:T(8,128)(2,1)} %copy.120) | copy-start | bytes 9437188
  214.6 0.8 copy-start.4
  433.8 15.2 %all-to-all-start.2 = ((bf16[8,1,16,768]{3,2,1,0:T(8,128)(2,1)}), bf16[8,1,16,768]{3,2,1,0:T(8,128)(2,1)S(1)}, u32[]{:S(2)}, u32[]{:S(2)}) async-start(bf16[8,1,16,768]{3,2,1,0:T(8,128)(2,1)} %bitcast.165), calls=%async_computation.3 | async-start | bytes 393216 | tf_op jit(solution)/shard_map/all_to_all | solution.py:136
Sparse Core Ops, SparseCore 0:
  214.8 218.9 reduce-scatter.1
